TPU v7x, 128 devices: a whole 4x4x4 slice. The times are simulated.
128 devices in a mesh: dp: 32 (over y, x, core), mp: 4 (over z).
Axes of the slice: x: 4, y: 4, z: 4, core: 2. Of those that a mesh axis runs over, the one named last changes fastest.
Arguments:
- hidden: bfloat16 [4096, 2560], P('dp', 'mp'), may hold values from -6 to 6
- norm_gain: bfloat16 [2560], replicated, may hold values from 0.5 to 1.5
- shared_gate: bfloat16 [2560, 3072], P(None, 'mp'), may hold values from -0.125 to 0.125
- shared_up: bfloat16 [2560, 3072], P(None, 'mp'), may hold values from -0.125 to 0.125
- shared_down: bfloat16 [3072, 2560], P('mp'), may hold values from -0.109375 to 0.109375
- expert_gate: bfloat16 [64, 2560, 1536], P('dp', None, 'mp'), may hold values from -0.125 to 0.125
- expert_up: bfloat16 [64, 2560, 1536], P('dp', None, 'mp'), may hold values from -0.125 to 0.125
- expert_down: bfloat16 [64, 1536, 2560], P('dp', 'mp'), may hold values from -0.15625 to 0.15625
- adapter_in: bfloat16 [64, 3072, 16], P('dp', 'mp'), may hold values from -0.109375 to 0.109375
- adapter_out: bfloat16 [64, 16, 2560], P('dp'), may hold values from -1.5 to 1.5
- active: int32 [16], replicated, may hold values from 0 to 63, as said below
- lengths: int32 [64], replicated, may hold values from 1 to 1024, 4096 in all
- request_adapter: int32 [64], replicated, may hold values from 0 to 15
- routes: int32 [4096, 6], P('dp'), may hold values from 0 to 63, all different within a row; in each aligned block of 128 rows (0 to 127, 128 to 255, ...) at most 16 rows name the same one
- route_weights: float32 [4096, 6], P('dp'), may hold values from 0.05 to 0.35
Outputs:
- layer_out: bfloat16 [4096, 2560], P('dp', 'mp')
Inputs may be any that keep to these rules, and one draw needn't show every extreme that they name: `active`: the entries are distinct. `routes`: within the 128 rows of one index of dp no expert is named more than 16 times, and that many is reached; a row names distinct experts.
All inputs are finite; a program needn't handle non-finite values.
Results may differ from a plain program's by a relative error of at most 0.015.
Values may be sent and summed in bfloat16 or wider, within the bound.
No kernel may reach another device: no remote copies, remote signals or barrier semaphores. Data moves between devices by JAX's collectives and lax.ppermute only.
A program may use at most 128 MiB of HBM per device.

v0:
```python
import jax
import jax.numpy as jnp
from jax import lax
from jax.sharding import PartitionSpec as P


def experts_apply(slots_in, expert_gate, expert_up, expert_down):
    gate_val = jnp.einsum(
        "sjcd,jdf->sjcf", slots_in, expert_gate, preferred_element_type=jnp.float32
    )
    up_val = jnp.einsum("sjcd,jdf->sjcf", slots_in, expert_up, preferred_element_type=jnp.float32)
    inner = (jax.nn.silu(gate_val) * up_val).astype(jnp.bfloat16)
    return jnp.einsum("sjcf,jfd->sjcd", inner, expert_down, preferred_element_type=jnp.float32)


def body(
    hidden,
    norm_gain,
    shared_gate,
    shared_up,
    shared_down,
    expert_gate,
    expert_up,
    expert_down,
    adapter_in,
    adapter_out,
    active,
    lengths,
    request_adapter,
    routes,
    route_weights,
):
    tok_rows = routes.shape[0]
    top_count = routes.shape[1]
    dp_count = lax.axis_size("dp")
    mp_count = lax.axis_size("mp")
    dp_index = lax.axis_index("dp")
    mp_index = lax.axis_index("mp")
    local_experts = expert_gate.shape[0]
    total_experts = local_experts * dp_count
    capacity = mp_count * max(1, tok_rows * top_count * 4 // (total_experts * mp_count * 3))
    col_width = hidden.shape[1]
    col_start = mp_index * col_width
    active_count = active.shape[0]
    rank_width = adapter_in.shape[2]
    local_adapters = adapter_in.shape[0]
    owned_ids = dp_index * local_adapters + jnp.arange(local_adapters, dtype=jnp.int32)
    selector = (active[:, None] == owned_ids[None, :]).astype(jnp.bfloat16)
    out_cols = lax.dynamic_slice_in_dim(adapter_out, col_start, col_width, axis=2)
    picked_in = jnp.einsum(
        "ji,isr->jsr", selector, adapter_in, preferred_element_type=jnp.float32
    ).astype(jnp.bfloat16)
    picked_out = jnp.einsum(
        "ji,ird->jrd", selector, out_cols, preferred_element_type=jnp.float32
    ).astype(jnp.bfloat16)
    picked_in, picked_out = lax.psum((picked_in, picked_out), "dp")
    gathered = lax.all_gather(hidden, "mp", axis=1, tiled=True)
    values = gathered.astype(jnp.float32)
    factor = lax.rsqrt(jnp.mean(values * values, axis=-1, keepdims=True) + 1e-06)
    normed = (values * factor * norm_gain.astype(jnp.float32)).astype(jnp.bfloat16)
    width = normed.shape[1]
    shared_lin = jnp.dot(normed, shared_gate, preferred_element_type=jnp.float32)
    shared_pre = jnp.dot(normed, shared_up, preferred_element_type=jnp.float32)
    shared_act = (jax.nn.silu(shared_lin) * shared_pre).astype(jnp.bfloat16)
    request_end = jnp.cumsum(lengths)
    positions = dp_index * tok_rows + jnp.arange(tok_rows, dtype=jnp.int32)
    request_of = jnp.sum((request_end[None, :] <= positions[:, None]).astype(jnp.int32), axis=1)
    request_hot = (
        request_of[:, None] == jnp.arange(lengths.shape[0], dtype=jnp.int32)[None, :]
    ).astype(jnp.int32)
    slot_of = jnp.sum(request_hot * request_adapter[None, :], axis=1)
    chosen = (slot_of[:, None] == jnp.arange(active_count, dtype=jnp.int32)[None, :]).astype(
        jnp.float32
    )
    in_matrix = jnp.transpose(picked_in, (1, 0, 2)).reshape(
        shared_act.shape[1], active_count * rank_width
    )
    lowrank = jnp.dot(shared_act, in_matrix, preferred_element_type=jnp.float32)
    lowrank_sel = jnp.sum(
        lowrank.reshape(tok_rows, active_count, rank_width) * chosen[:, :, None], axis=1
    )
    lowrank_sel = lax.psum(lowrank_sel, "mp")
    lowrank = (chosen[:, :, None] * lowrank_sel[:, None, :]).reshape(
        tok_rows, active_count * rank_width
    )
    adapted = jnp.dot(
        lowrank,
        picked_out.reshape(active_count * rank_width, col_width).astype(jnp.float32),
        precision=lax.Precision.HIGHEST,
    )
    flat_routes = routes.reshape(-1)
    expert_hot = (
        flat_routes[:, None] == jnp.arange(total_experts, dtype=jnp.int32)[None, :]
    ).astype(jnp.int32)
    earlier = jnp.cumsum(expert_hot, axis=0) - expert_hot
    position = jnp.sum(earlier * expert_hot, axis=1)
    slot_index = (flat_routes * capacity + position).reshape(tok_rows, top_count)
    slot_count = total_experts * capacity
    slot_hit = slot_index[:, :, None] == jnp.arange(slot_count, dtype=jnp.int32)[None, None, :]
    dispatch = jnp.any(slot_hit, axis=1).astype(jnp.bfloat16)
    send_rows = jnp.einsum(
        "ts,td->sd", dispatch, normed, preferred_element_type=jnp.float32
    ).astype(jnp.bfloat16)
    send_rows = send_rows.reshape(dp_count, local_experts, capacity, width)
    returned = lax.all_to_all(
        experts_apply(
            lax.all_to_all(send_rows, "dp", split_axis=0, concat_axis=0, tiled=True),
            expert_gate,
            expert_up,
            expert_down,
        ).astype(jnp.bfloat16),
        "dp",
        split_axis=0,
        concat_axis=0,
        tiled=True,
    )
    returned = returned.reshape(slot_count, width)
    combine = jnp.sum(jnp.where(slot_hit, route_weights[:, :, None], 0.0), axis=1)
    combine_hi = combine.astype(jnp.bfloat16)
    combine_lo = (combine - combine_hi.astype(jnp.float32)).astype(jnp.bfloat16)
    routed = jnp.dot(combine_hi, returned, preferred_element_type=jnp.float32) + jnp.dot(
        combine_lo, returned, preferred_element_type=jnp.float32
    )
    partial_out = jnp.dot(shared_act, shared_down, preferred_element_type=jnp.float32) + routed
    own_cols = lax.dynamic_slice_in_dim(partial_out, col_start, col_width, axis=1) + adapted
    partial_out = lax.dynamic_update_slice_in_dim(partial_out, own_cols, col_start, axis=1)
    return lax.psum_scatter(partial_out.astype(jnp.bfloat16), "mp", scatter_dimension=1, tiled=True)


def solution(mesh):
    in_specs = (
        P("dp", "mp"),
        P(),
        P(None, "mp"),
        P(None, "mp"),
        P("mp", None),
        P("dp", None, "mp"),
        P("dp", None, "mp"),
        P("dp", "mp", None),
        P("dp", "mp", None),
        P("dp", None, None),
        P(),
        P(),
        P(),
        P("dp", None),
        P("dp", None),
    )
    out_specs = P("dp", "mp")
    return jax.shard_map(body, mesh=mesh, in_specs=in_specs, out_specs=out_specs, check_vma=False)
```

profile of v0, /device:TPU:0, one launch (start us, length us, event | category | flops | bytes accessed | tf_op | source)
XLA Modules:
  0.0 315.9 jit_solution(4285871344129331172)
XLA Ops:
  6.5 0.0 copy-start
  6.5 0.8 copy.60
  7.4 0.1 eq.85
  7.5 0.1 eq.81
  7.7 1.8 reduce-window.18
  9.5 0.3 slice_reduce_fusion
  9.8 0.1 fusion.34
  9.9 0.1 reduce_sum.58
  10.1 0.1 copy.63
  10.1 0.7 multiply_add_fusion
  10.8 0.5 fusion.9
  11.3 14.9 %all_gather.3 = bf16[128,2560]{1,0:T(8,128)(2,1)S(1)} all-gather(bf16[128,640]{1,0:T(8,128)(2,1)} %param.15), channel_id=1, replica_groups=mesh['dp'=32,'mp'=4] {'mp'}, dimensions={1}, use_global_device_ids=true | all-gather | bytes 819200 | tf_op jit(solution)/shard_map/all_gather | solution.py:57
  26.2 0.2 fusion.22
  26.5 0.7 convert_element_type.64
  27.2 1.6 convolution_convert_fusion.1
  28.8 0.0 copy-start.8
  28.8 69.5 %all_to_all.10 = bf16[32,2,16,2560]{3,2,1,0:T(8,128)(2,1)S(1)} all-to-all(bf16[32,2,16,2560]{3,2,1,0:T(8,128)(2,1)S(1)} %bitcast.98), channel_id=1, replica_groups=mesh['dp'=32,'mp'=4] {'dp'}, dimensions={0} | all-to-all | bytes 10485760 | tf_op jit(solution)/shard_map/all_to_all | solution.py:107
  98.3 0.0 copy-start.1
  98.3 2.3 copy-done.1
  100.6 0.0 copy-done.8
  100.6 2.9 fusion.3
  103.5 12.8 %fusion = bf16[32,2,16,2560]{3,2,0,1:T(8,128)(2,1)} fusion(bf16[2,384,2560]{2,1,0:T(8,128)(2,1)} %param.22, f32[2,32,16,384]{3,2,1,0:T(8,128)S(1)} %fusion.3, bf16[2,2560,384]{2,1,0:T(8,128)(2,1)} %param.21, bf16[32,2,16,2560]{3,2,1,0:T(8,128)(2,1)} %copy-done.1), kind=kOutput, calls=%fused_computation.2 | convolution fusion | flops 4031512576 | bytes 19922944 | tf_op jit(solution)/shard_map/sjcf,jfd->sjcd/dot_general | solution.py:13
  116.3 5.3 %copy.66 = bf16[32,2,16,2560]{3,2,1,0:T(8,128)(2,1)} copy(bf16[32,2,16,2560]{3,2,0,1:T(8,128)(2,1)} %fusion) | data formatting | bytes 10485760 | tf_op jit(solution)/shard_map/convert_element_type | solution.py:111
  121.5 0.0 copy-start.5
  121.5 5.0 %all-to-all-start.1 = ((bf16[32,2,16,2560]{3,2,1,0:T(8,128)(2,1)}), bf16[32,2,16,2560]{3,2,1,0:T(8,128)(2,1)}, u32[]{:S(2)}, u32[]{:S(2)}) async-start(bf16[32,2,16,2560]{3,2,1,0:T(8,128)(2,1)} %copy.66), calls=%async_computation.1 | async-start | bytes 10485760 | tf_op jit(solution)/shard_map/all_to_all | solution.py:105
  126.6 0.0 all-reduce.3.cloned.1.call-start
  126.6 0.0 copy-done.4
  126.6 0.0 copy-done.6
  126.6 0.4 fusion.25
  127.1 0.9 copy.95
  127.9 0.0 copy-done
  128.0 1.1 convolution_convert_fusion.3
  129.1 0.0 all-reduce.3.cloned.1.call-update
  129.1 0.2 reduce-scatter.4.cloned.1.call-start
  129.3 0.0 copy-done.7
  129.4 0.1 copy.67
  129.5 0.1 reduce-window.20
  129.5 0.1 reduce.1
  129.7 0.0 copy-start.9
  129.7 0.1 convert_reduce_fusion
  129.8 0.0 copy-done.10
  129.8 0.1 select_reduce_fusion.1
  129.9 0.0 copy-done.5
  129.9 0.4 select_reduce_fusion
  130.3 3.2 fusion.57
  133.5 0.0 copy-done.9
  133.5 0.0 copy-start.2
  133.5 0.8 fusion.26
  134.3 1.3 copy-done.2
  135.6 0.7 fusion.59
  136.3 131.0 %all-reduce.3.cloned.1.call-done = (bf16[16,16,640]{2,0,1:T(8,128)(2,1)}, bf16[16,16,768]{2,1,0:T(8,128)(2,1)}) async-done(((bf16[16,16,640]{2,0,1:T(8,128)(2,1)}, bf16[16,16,768]{2,1,0:T(8,128)(2,1)}), (bf16[16,16,640]{2,0,1:T(8,128)(2,1)}, bf16[16,16,768]{2,1,0:T(8,128)(2,1)})) %all-reduce.3.cloned.1.call-update) | async-done | bytes 720912 | tf_op jit(solution)/shard_map/psum | solution.py:56
  267.3 1.3 fusion.29
  268.6 10.8 %psum.22 = f32[128,16]{0,1:T(8,128)S(1)} all-reduce(f32[128,16]{0,1:T(8,128)S(1)} %fusion.29), channel_id=1, replica_groups=mesh['dp'=32,'mp'=4] {'mp'}, use_global_device_ids=true, to_apply=%region_11.12 | all-reduce | flops 2048 | bytes 16384 | tf_op jit(solution)/shard_map/psum | solution.py:82
  279.4 0.0 all-to-all-done.1
  279.4 3.3 %fusion.39 = f32[128,2560]{1,0:T(8,128)S(1)} fusion(bf16[1024,2560]{1,0:T(8,128)(2,1)} %bitcast.11, f32[128,1024]{1,0:T(8,128)S(1)} %select_reduce_fusion), kind=kOutput, calls=%fused_computation.53 | convolution fusion | flops 671219712 | bytes 7077888 | tf_op jit(solution)/shard_map/dot_general | solution.py:121
  282.7 0.0 copy-start.3
  282.7 3.5 %fusion.8 = f32[128,2560]{1,0:T(8,128)S(1)} fusion(f32[128,2560]{1,0:T(8,128)S(1)} %fusion.59, f32[128,2560]{1,0:T(8,128)S(1)} %fusion.39, bf16[1024,2560]{1,0:T(8,128)(2,1)} %bitcast.11, f32[128,1024]{1,0:T(8,128)S(1)} %select_reduce_fusion), kind=kOutput, calls=%fused_computation.11 | convolution fusion | flops 672268288 | bytes 9699328 | tf_op jit(solution)/shard_map/dot_general | solution.py:121
  286.2 0.0 copy-done.3
  286.2 0.4 fusion.28
  286.6 0.1 convert_element_type.80
  286.7 1.1 copy.75
  287.8 0.0 reduce-scatter.4.cloned.1.call-update
  287.8 19.6 %reduce-scatter.4.cloned.1.call-done = bf16[640,128]{1,0:T(8,128)(2,1)} async-done(((bf16[2560,128]{1,0:T(8,128)(2,1)}), bf16[640,128]{1,0:T(8,128)(2,1)}) %reduce-scatter.4.cloned.1.call-update) | async-done | bytes 163856
  307.4 1.7 copy.76
  (11 shorter events, 0.1 us)
Async XLA Ops:
  6.5 121.4 %copy-start = (bf16[2,16,2560]{2,1,0:T(8,128)(2,1)S(1)}, bf16[2,16,2560]{2,1,0:T(8,128)(2,1)}, u32[]{:S(2)}) copy-start(bf16[2,16,2560]{2,1,0:T(8,128)(2,1)} %param.24) | copy-start | bytes 491524
  28.8 71.8 %copy-start.8 = (bf16[2,2560,384]{2,1,0:T(8,128)(2,1)S(1)}, bf16[2,2560,384]{2,1,0:T(8,128)(2,1)}, u32[]{:S(2)}) copy-start(bf16[2,2560,384]{2,1,0:T(8,128)(2,1)} %param.20) | copy-start | bytes 11796484
  98.3 2.3 copy-start.1
  121.5 5.1 %copy-start.4 = (bf16[2,768,16]{1,2,0:T(8,128)(2,1)S(1)}, bf16[2,768,16]{1,2,0:T(8,128)(2,1)}, u32[]{:S(2)}) copy-start(bf16[2,768,16]{1,2,0:T(8,128)(2,1)} %param.23) | copy-start | bytes 147460
  121.5 5.1 %copy-start.6 = (s32[16]{0:T(128)S(1)}, s32[16]{0:T(128)}, u32[]{:S(2)}) copy-start(s32[16]{0:T(128)} %param.25) | copy-start | bytes 196
  121.5 7.8 %copy-start.7 = (s32[64]{0:T(128)S(1)}, s32[64]{0:T(128)}, u32[]{:S(2)}) copy-start(s32[64]{0:T(128)} %param.26) | copy-start | bytes 772
  121.5 8.2 %copy-start.10 = (s32[64]{0:T(128)S(1)}, s32[64]{0:T(128)}, u32[]{:S(2)}) copy-start(s32[64]{0:T(128)} %param.27) | copy-start | bytes 772
  121.5 8.3 %copy-start.5 = (f32[128,6]{0,1:T(8,128)S(1)}, f32[128,6]{0,1:T(8,128)}, u32[]{:S(2)}) copy-start(f32[128,6]{0,1:T(8,128)} %param.29) | copy-start | bytes 9220
  121.5 157.8 %all-to-all-start.1 = ((bf16[32,2,16,2560]{3,2,1,0:T(8,128)(2,1)}), bf16[32,2,16,2560]{3,2,1,0:T(8,128)(2,1)}, u32[]{:S(2)}, u32[]{:S(2)}) async-start(bf16[32,2,16,2560]{3,2,1,0:T(8,128)(2,1)} %copy.66), calls=%async_computation.1 | async-start | bytes 10485760 | tf_op jit(solution)/shard_map/all_to_all | solution.py:105
  126.6 140.7 %all-reduce.3.cloned.1.call-start = ((), (), s32[]{:S(2)}) async-start(), calls=%async_computation.4 | async-start | bytes 1441792 | tf_op jit(solution)/shard_map/psum | solution.py:56
  129.1 178.2 %reduce-scatter.4.cloned.1.call-start = ((), (), s32[]{:S(2)}) async-start(), calls=%async_computation.3 | async-start | bytes 819200
  129.7 3.8 %copy-start.9 = (bf16[2560,768]{1,0:T(8,128)(2,1)S(1)}, bf16[2560,768]{1,0:T(8,128)(2,1)}, u32[]{:S(2)}) copy-start(bf16[2560,768]{1,0:T(8,128)(2,1)} %param.18) | copy-start | bytes 11796484
  133.5 2.1 copy-start.2
  282.7 3.5 %copy-start.3 = (bf16[16,16,640]{2,0,1:T(8,128)(2,1)S(1)}, bf16[16,16,640]{2,0,1:T(8,128)(2,1)}, u32[]{:S(2)}) copy-start(bf16[16,16,640]{2,0,1:T(8,128)(2,1)} %get-tuple-element.5) | copy-start | bytes 983044
Sparse Core Ops, SparseCore 0:
  130.8 136.4 all-reduce.2
  287.9 19.4 reduce-scatter.3
where the time goes:
time: 316 us
  waiting for transfers between devices  151 us (48%)
  blocking collectives  95.2 us (30%)
  matrix products  31.9 us (10%)
  local copies, waits for them, and re-layouts  14.3 us (5%)
  between operations  13.7 us (4%)
  starting transfers between devices  5.27 us (2%)
  other arithmetic  4.99 us (2%)
    psum x1, waiting for transfers between devices, body(): picked_in, picked_out = lax.psum((picked_in, picked_out), 'dp')  131 us
    all_to_all x1, blocking collectives, body(): lax.all_to_all(send_rows, 'dp', split_axis=0, concat_axis=0, tiled=True)  69.5 us
    unnamed x3, waiting for transfers between devices  19.6 us
    all_gather x1, blocking collectives, body(): gathered = lax.all_gather(hidden, 'mp', axis=1, tiled=True)  14.9 us
    dot_general x1, matrix products, experts_apply(): jnp.einsum('sjcf,jfd->sjcd', inner, expert_down, preferred_element_type=j...  12.8 us
    psum x1, blocking collectives, body(): lowrank_sel = lax.psum(lowrank_sel, 'mp')  10.8 us
    unnamed x25, local copies, waits for them, and re-layouts  7.3 us
  transfers between devices with their start and end apart: 3, of which 2 were waited for; matrix products, arithmetic and copies ran while one was open for 3% of the time, Pallas kernels for 0%

commit v1 on v0

--- a/solution.py
+++ b/solution.py
@@ -79,7 +79,7 @@
     lowrank_sel = jnp.sum(
         lowrank.reshape(tok_rows, active_count, rank_width) * chosen[:, :, None], axis=1
     )
-    lowrank_sel = lax.psum(lowrank_sel, "mp")
+    lowrank_sel = jnp.sum(lax.all_gather(lowrank_sel, "mp"), axis=0)
     lowrank = (chosen[:, :, None] * lowrank_sel[:, None, :]).reshape(
         tok_rows, active_count * rank_width
     )

time: 316 us -> 320 us (1.013)
    all_gather x0 -> x1, blocking collectives: none -> 12.4 us  [body(): lowrank_sel = jnp.sum(lax.all_gather(lowrank_sel, 'mp'), axis=0)]
    psum x1 -> x0, blocking collectives: 10.8 us -> none  [body(): lowrank_sel = lax.psum(lowrank_sel, 'mp')]
where the time goes in v1:
time: 320 us; the launch traced here: 319 us
  waiting for transfers between devices  152 us (48%)
  blocking collectives  96.8 us (30%)
  matrix products  31.9 us (10%)
  local copies, waits for them, and re-layouts  14.3 us (4%)
  between operations  13.7 us (4%)
  starting transfers between devices  5.27 us (2%)
  other arithmetic  5.01 us (2%)
    psum x1, waiting for transfers between devices, body(): picked_in, picked_out = lax.psum((picked_in, picked_out), 'dp')  131 us
    all_to_all x1, blocking collectives, body(): lax.all_to_all(send_rows, 'dp', split_axis=0, concat_axis=0, tiled=True)  69.5 us
    unnamed x3, waiting for transfers between devices  21.3 us
    all_gather x1, blocking collectives, body(): gathered = lax.all_gather(hidden, 'mp', axis=1, tiled=True)  14.9 us
    dot_general x1, matrix products, experts_apply(): jnp.einsum('sjcf,jfd->sjcd', inner, expert_down, preferred_element_type=j...  12.8 us
    all_gather x1, blocking collectives, body(): lowrank_sel = jnp.sum(lax.all_gather(lowrank_sel, 'mp'), axis=0)  12.4 us
    unnamed x25, local copies, waits for them, and re-layouts  7.3 us
  transfers between devices with their start and end apart: 3, of which 2 were waited for; matrix products, arithmetic and copies ran while one was open for 3% of the time, Pallas kernels for 0%

profile of v1, /device:TPU:0, one launch (start us, length us, event | category | flops | bytes accessed | tf_op | source)
XLA Modules:
  0.0 319.2 jit_solution(14107938899039969940)
XLA Ops:
  6.5 0.0 copy-start
  6.5 0.8 copy.60
  7.4 0.1 eq.85
  7.5 0.1 eq.81
  7.7 1.8 reduce-window.18
  9.5 0.3 slice_reduce_fusion
  9.8 0.1 fusion.34
  9.9 0.1 reduce_sum.67
  10.1 0.1 copy.63
  10.1 0.7 multiply_add_fusion
  10.8 0.5 fusion.9
  11.3 14.9 %all_gather.9 = bf16[128,2560]{1,0:T(8,128)(2,1)S(1)} all-gather(bf16[128,640]{1,0:T(8,128)(2,1)} %param.15), channel_id=1, replica_groups=mesh['dp'=32,'mp'=4] {'mp'}, dimensions={1}, use_global_device_ids=true | all-gather | bytes 819200 | tf_op jit(solution)/shard_map/all_gather | solution.py:57
  26.2 0.2 fusion.22
  26.5 0.7 convert_element_type.64
  27.2 1.6 convolution_convert_fusion.1
  28.8 0.0 copy-start.8
  28.8 69.5 %all_to_all.10 = bf16[32,2,16,2560]{3,2,1,0:T(8,128)(2,1)S(1)} all-to-all(bf16[32,2,16,2560]{3,2,1,0:T(8,128)(2,1)S(1)} %bitcast.100), channel_id=1, replica_groups=mesh['dp'=32,'mp'=4] {'dp'}, dimensions={0} | all-to-all | bytes 10485760 | tf_op jit(solution)/shard_map/all_to_all | solution.py:107
  98.3 0.0 copy-start.1
  98.3 2.3 copy-done.1
  100.6 0.0 copy-done.8
  100.6 2.9 fusion.3
  103.5 12.8 %fusion = bf16[32,2,16,2560]{3,2,0,1:T(8,128)(2,1)} fusion(bf16[2,384,2560]{2,1,0:T(8,128)(2,1)} %param.22, f32[2,32,16,384]{3,2,1,0:T(8,128)S(1)} %fusion.3, bf16[2,2560,384]{2,1,0:T(8,128)(2,1)} %param.21, bf16[32,2,16,2560]{3,2,1,0:T(8,128)(2,1)} %copy-done.1), kind=kOutput, calls=%fused_computation.2 | convolution fusion | flops 4031512576 | bytes 19922944 | tf_op jit(solution)/shard_map/sjcf,jfd->sjcd/dot_general | solution.py:13
  116.3 5.3 %copy.66 = bf16[32,2,16,2560]{3,2,1,0:T(8,128)(2,1)} copy(bf16[32,2,16,2560]{3,2,0,1:T(8,128)(2,1)} %fusion) | data formatting | bytes 10485760 | tf_op jit(solution)/shard_map/convert_element_type | solution.py:111
  121.5 0.0 copy-start.5
  121.5 5.0 %all-to-all-start.1 = ((bf16[32,2,16,2560]{3,2,1,0:T(8,128)(2,1)}), bf16[32,2,16,2560]{3,2,1,0:T(8,128)(2,1)}, u32[]{:S(2)}, u32[]{:S(2)}) async-start(bf16[32,2,16,2560]{3,2,1,0:T(8,128)(2,1)} %copy.66), calls=%async_computation.1 | async-start | bytes 10485760 | tf_op jit(solution)/shard_map/all_to_all | solution.py:105
  126.6 0.0 all-reduce.3.cloned.1.call-start
  126.6 0.0 copy-done.4
  126.6 0.0 copy-done.6
  126.6 0.4 fusion.25
  127.1 0.9 copy.95
  127.9 0.0 copy-done
  128.0 1.1 convolution_convert_fusion.3
  129.1 0.0 all-reduce.3.cloned.1.call-update
  129.1 0.2 reduce-scatter.4.cloned.1.call-start
  129.3 0.0 copy-done.7
  129.4 0.1 copy.67
  129.5 0.1 reduce-window.20
  129.5 0.1 reduce.1
  129.7 0.0 copy-start.9
  129.7 0.1 convert_reduce_fusion
  129.8 0.0 copy-done.10
  129.8 0.1 select_reduce_fusion.1
  129.9 0.0 copy-done.5
  129.9 0.4 select_reduce_fusion
  130.3 3.2 fusion.57
  133.5 0.0 copy-done.9
  133.5 0.0 copy-start.2
  133.5 0.8 fusion.26
  134.3 1.3 copy-done.2
  135.6 0.7 fusion.59
  136.3 131.0 %all-reduce.3.cloned.1.call-done = (bf16[16,16,640]{2,0,1:T(8,128)(2,1)}, bf16[16,16,768]{2,1,0:T(8,128)(2,1)}) async-done(((bf16[16,16,640]{2,0,1:T(8,128)(2,1)}, bf16[16,16,768]{2,1,0:T(8,128)(2,1)}), (bf16[16,16,640]{2,0,1:T(8,128)(2,1)}, bf16[16,16,768]{2,1,0:T(8,128)(2,1)})) %all-reduce.3.cloned.1.call-update) | async-done | bytes 720912 | tf_op jit(solution)/shard_map/psum | solution.py:56
  267.3 1.3 fusion.29
  268.6 12.4 %all-gather = f32[512,16]{0,1:T(8,128)S(1)} all-gather(f32[128,16]{0,1:T(8,128)S(1)} %fusion.29), channel_id=2, replica_groups=mesh['dp'=32,'mp'=4] {'mp'}, dimensions={0}, use_global_device_ids=true | all-gather | bytes 40960 | tf_op jit(solution)/shard_map/all_gather | solution.py:82
  281.0 0.0 all-to-all-done.1
  281.0 3.3 %fusion.39 = f32[128,2560]{1,0:T(8,128)S(1)} fusion(bf16[1024,2560]{1,0:T(8,128)(2,1)} %bitcast.11, f32[128,1024]{1,0:T(8,128)S(1)} %select_reduce_fusion), kind=kOutput, calls=%fused_computation.53 | convolution fusion | flops 671219712 | bytes 7077888 | tf_op jit(solution)/shard_map/dot_general | solution.py:121
  284.4 0.0 copy-start.3
  284.4 3.5 %fusion.8 = f32[128,2560]{1,0:T(8,128)S(1)} fusion(f32[128,2560]{1,0:T(8,128)S(1)} %fusion.59, f32[128,2560]{1,0:T(8,128)S(1)} %fusion.39, bf16[1024,2560]{1,0:T(8,128)(2,1)} %bitcast.11, f32[128,1024]{1,0:T(8,128)S(1)} %select_reduce_fusion), kind=kOutput, calls=%fused_computation.11 | convolution fusion | flops 672268288 | bytes 9699328 | tf_op jit(solution)/shard_map/dot_general | solution.py:121
  287.9 0.0 copy-done.3
  287.9 0.4 fusion.28
  288.2 0.1 convert_element_type.80
  288.3 1.1 copy.75
  289.4 0.0 reduce-scatter.4.cloned.1.call-update
  289.4 21.3 %reduce-scatter.4.cloned.1.call-done = bf16[640,128]{1,0:T(8,128)(2,1)} async-done(((bf16[2560,128]{1,0:T(8,128)(2,1)}), bf16[640,128]{1,0:T(8,128)(2,1)}) %reduce-scatter.4.cloned.1.call-update) | async-done | bytes 163856
  310.7 1.7 copy.76
  (13 shorter events, 0.1 us)
Async XLA Ops:
  6.5 121.4 %copy-start = (bf16[2,16,2560]{2,1,0:T(8,128)(2,1)S(1)}, bf16[2,16,2560]{2,1,0:T(8,128)(2,1)}, u32[]{:S(2)}) copy-start(bf16[2,16,2560]{2,1,0:T(8,128)(2,1)} %param.24) | copy-start | bytes 491524
  28.8 71.8 %copy-start.8 = (bf16[2,2560,384]{2,1,0:T(8,128)(2,1)S(1)}, bf16[2,2560,384]{2,1,0:T(8,128)(2,1)}, u32[]{:S(2)}) copy-start(bf16[2,2560,384]{2,1,0:T(8,128)(2,1)} %param.20) | copy-start | bytes 11796484
  98.3 2.3 copy-start.1
  121.5 5.1 %copy-start.4 = (bf16[2,768,16]{1,2,0:T(8,128)(2,1)S(1)}, bf16[2,768,16]{1,2,0:T(8,128)(2,1)}, u32[]{:S(2)}) copy-start(bf16[2,768,16]{1,2,0:T(8,128)(2,1)} %param.23) | copy-start | bytes 147460
  121.5 5.1 %copy-start.6 = (s32[16]{0:T(128)S(1)}, s32[16]{0:T(128)}, u32[]{:S(2)}) copy-start(s32[16]{0:T(128)} %param.25) | copy-start | bytes 196
  121.5 7.8 %copy-start.7 = (s32[64]{0:T(128)S(1)}, s32[64]{0:T(128)}, u32[]{:S(2)}) copy-start(s32[64]{0:T(128)} %param.26) | copy-start | bytes 772
  121.5 8.2 %copy-start.10 = (s32[64]{0:T(128)S(1)}, s32[64]{0:T(128)}, u32[]{:S(2)}) copy-start(s32[64]{0:T(128)} %param.27) | copy-start | bytes 772
  121.5 8.3 %copy-start.5 = (f32[128,6]{0,1:T(8,128)S(1)}, f32[128,6]{0,1:T(8,128)}, u32[]{:S(2)}) copy-start(f32[128,6]{0,1:T(8,128)} %param.29) | copy-start | bytes 9220
  121.5 159.5 %all-to-all-start.1 = ((bf16[32,2,16,2560]{3,2,1,0:T(8,128)(2,1)}), bf16[32,2,16,2560]{3,2,1,0:T(8,128)(2,1)}, u32[]{:S(2)}, u32[]{:S(2)}) async-start(bf16[32,2,16,2560]{3,2,1,0:T(8,128)(2,1)} %copy.66), calls=%async_computation.1 | async-start | bytes 10485760 | tf_op jit(solution)/shard_map/all_to_all | solution.py:105
  126.6 140.7 %all-reduce.3.cloned.1.call-start = ((), (), s32[]{:S(2)}) async-start(), calls=%async_computation.4 | async-start | bytes 1441792 | tf_op jit(solution)/shard_map/psum | solution.py:56
  129.1 181.6 %reduce-scatter.4.cloned.1.call-start = ((), (), s32[]{:S(2)}) async-start(), calls=%async_computation.3 | async-start | bytes 819200
  129.7 3.8 %copy-start.9 = (bf16[2560,768]{1,0:T(8,128)(2,1)S(1)}, bf16[2560,768]{1,0:T(8,128)(2,1)}, u32[]{:S(2)}) copy-start(bf16[2560,768]{1,0:T(8,128)(2,1)} %param.18) | copy-start | bytes 11796484
  133.5 2.1 copy-start.2
  284.4 3.5 %copy-start.3 = (bf16[16,16,640]{2,0,1:T(8,128)(2,1)S(1)}, bf16[16,16,640]{2,0,1:T(8,128)(2,1)}, u32[]{:S(2)}) copy-start(bf16[16,16,640]{2,0,1:T(8,128)(2,1)} %get-tuple-element.5) | copy-start | bytes 983044
Sparse Core Ops, SparseCore 0:
  130.8 136.4 all-reduce.2
  289.5 21.0 reduce-scatter.3
